TPU v7x, 256 devices: a whole 4x4x8 slice. The times are simulated.
256 devices in a mesh: blk: 32 (over y, x, z_hi), grp: 8 (over z_lo, core).
Axes of the slice: x: 4, y: 4, z: 8 (z_hi: 2, z_lo: 4; z = z_hi * 4 + z_lo), core: 2. Of those that a mesh axis runs over, the one named last changes fastest.
Arguments:
- x_blocks: bfloat16 [4096, 128, 128], P(('blk', 'grp')), may hold values from -0.59765625 to 0.59765625
- pair_left: int32 [32, 8, 32, 12], P('blk', 'grp'), may hold values from 0 to 127
- pair_right: int32 [32, 8, 32, 12], P('blk', 'grp'), may hold values from 0 to 127
- pair_target: int32 [32, 8, 32, 12], P('blk', 'grp'), may hold values from 0 to 3
Outputs:
- c_blocks: bfloat16 [32, 8, 4, 128, 128], P('blk', 'grp')
All inputs are finite; a program needn't handle non-finite values.
Results may differ from a plain program's by a relative error of at most 0.001.
Values may be sent and summed in bfloat16 or wider, within the bound.
No kernel may reach another device: no remote copies, remote signals or barrier semaphores. Data moves between devices by JAX's collectives and lax.ppermute only.
A program may use at most 64 MiB of HBM per device.

v0:
```python
import jax
import jax.numpy as jnp
from jax import lax
from jax.sharding import PartitionSpec as P

CS = 4


def from_behind(block, axis, distance):
    devices = range(lax.axis_size(axis))
    route = [((i - distance) % len(devices), i) for i in devices]
    return lax.ppermute(block, axis, route)


def per_device(x_blocks, pair_left, pair_right, pair_target):
    gathered = lax.all_gather(x_blocks, "grp", axis=0, tiled=True)
    group_count = lax.axis_size("blk")
    left_all = pair_left[0, 0]
    right_all = pair_right[0, 0]
    target_all = pair_target[0, 0]
    block_order = x_blocks.shape[1]
    panel_count = gathered.shape[0]
    pair_count = left_all.shape[1]
    flat_panel = gathered.reshape(panel_count, block_order * block_order)

    def partial_value(turn_index):
        left_index = lax.dynamic_index_in_dim(left_all, turn_index, 0, keepdims=False)
        right_index = lax.dynamic_index_in_dim(right_all, turn_index, 0, keepdims=False)
        target_index = lax.dynamic_index_in_dim(target_all, turn_index, 0, keepdims=False)
        both_index = jnp.concatenate([left_index, right_index])
        one_hot = (both_index[:, None] == jnp.arange(panel_count, dtype=jnp.int32)[None, :]).astype(
            jnp.bfloat16
        )
        picked = jnp.dot(one_hot, flat_panel, preferred_element_type=jnp.float32).astype(
            jnp.bfloat16
        )
        picked = picked.reshape(2 * pair_count, block_order, block_order)
        left_tiles = picked[:pair_count]
        right_tiles = picked[pair_count:]
        product = jnp.einsum(
            "pxy,pxz->pyz", left_tiles, right_tiles, preferred_element_type=jnp.float32
        )
        selector = (target_index[:, None] == jnp.arange(CS, dtype=jnp.int32)[None, :]).astype(
            jnp.float32
        )
        return jnp.einsum("pc,pyz->cyz", selector, product, precision=lax.Precision.HIGHEST)

    def advance(turn_index, carried):
        arrived = from_behind(carried, "blk", 1)
        return arrived + partial_value(turn_index)

    summed = lax.fori_loop(1, group_count, advance, partial_value(0))
    return summed.astype(jnp.bfloat16).reshape(1, 1, CS, block_order, block_order)


def solution(mesh):
    return jax.shard_map(
        per_device,
        mesh=mesh,
        in_specs=(
            P(("blk", "grp"), None, None),
            P("blk", "grp", None, None),
            P("blk", "grp", None, None),
            P("blk", "grp", None, None),
        ),
        out_specs=P("blk", "grp", None, None, None),
        check_vma=False,
    )
```

profile of v0, /device:TPU:120, one launch (start us, length us, event | category | flops | bytes accessed | tf_op | source)
XLA Modules:
  0.0 671.8 jit_solution(15409390500098320005)
XLA Ops:
  11.9 50.7 %all-gather.2.cloned.1.call-done = bf16[128,128,128]{2,1,0:T(8,128)(2,1)} async-done(((bf16[16,128,128]{2,1,0:T(8,128)(2,1)}), bf16[128,128,128]{2,1,0:T(8,128)(2,1)}) %all-gather.2.cloned.1.call-update) | async-done | bytes 4194320 | tf_op jit(solution)/shard_map/all_gather | solution.py:16
  62.6 7.8 %copy.37 = bf16[16,8,128,128]{3,1,2,0:T(8,128)(2,1)} copy(bf16[16,8,128,128]{3,2,1,0:T(8,128)(2,1)} %bitcast.57) | data formatting | bytes 8388608
  74.3 589.9 %while.15 = (s32[]{:T(128)}, f32[4,128,128]{2,0,1:T(4,128)S(1)}, s32[32,12]{1,0:T(8,128)S(1)}, s32[32,12]{1,0:T(8,128)S(1)}, s32[32,12]{1,0:T(8,128)S(1)}, /*ind...) while((s32[]{:T(128)}, f32[4,128,128]{2,0,1:T(4,128)S(1)}, s32[32,12]{1,0:T(8,128)S(1)}, ...), condition=%wide.region_1.2_spmd, body=%wide.region_0.1_spmd.sunk | while | flops 160894032 | bytes 12583719 | solution.py:52
  80.0 11.3 %collective-permute-done = f32[4,128,128]{2,0,1:T(4,128)S(1)} collective-permute-done((f32[4,128,128]{2,0,1:T(4,128)S(1)}, f32[4,128,128]{2,0,1:T(4,128)S(1)}, u32[]{:S(2)}, u32[]{:S(2)}) %collective-permute-start) | collective-permute-done | bytes 262176 | tf_op jit(solution)/shard_map/while/body/eval_jaxpr/ppermute | solution.py:12
  92.4 2.9 convolution_convert_fusion.3
  96.0 15.9 %collective-permute-done = f32[4,128,128]{2,0,1:T(4,128)S(1)} collective-permute-done((f32[4,128,128]{2,0,1:T(4,128)S(1)}, f32[4,128,128]{2,0,1:T(4,128)S(1)}, u32[]{:S(2)}, u32[]{:S(2)}) %collective-permute-start) | collective-permute-done | bytes 262176 | tf_op jit(solution)/shard_map/while/body/eval_jaxpr/ppermute | solution.py:12
  113.0 2.9 convolution_convert_fusion.3
  116.6 16.1 %collective-permute-done = f32[4,128,128]{2,0,1:T(4,128)S(1)} collective-permute-done((f32[4,128,128]{2,0,1:T(4,128)S(1)}, f32[4,128,128]{2,0,1:T(4,128)S(1)}, u32[]{:S(2)}, u32[]{:S(2)}) %collective-permute-start) | collective-permute-done | bytes 262176 | tf_op jit(solution)/shard_map/while/body/eval_jaxpr/ppermute | solution.py:12
  133.8 2.9 convolution_convert_fusion.3
  137.3 12.8 %collective-permute-done = f32[4,128,128]{2,0,1:T(4,128)S(1)} collective-permute-done((f32[4,128,128]{2,0,1:T(4,128)S(1)}, f32[4,128,128]{2,0,1:T(4,128)S(1)}, u32[]{:S(2)}, u32[]{:S(2)}) %collective-permute-start) | collective-permute-done | bytes 262176 | tf_op jit(solution)/shard_map/while/body/eval_jaxpr/ppermute | solution.py:12
  151.3 2.9 convolution_convert_fusion.3
  154.8 17.2 %collective-permute-done = f32[4,128,128]{2,0,1:T(4,128)S(1)} collective-permute-done((f32[4,128,128]{2,0,1:T(4,128)S(1)}, f32[4,128,128]{2,0,1:T(4,128)S(1)}, u32[]{:S(2)}, u32[]{:S(2)}) %collective-permute-start) | collective-permute-done | bytes 262176 | tf_op jit(solution)/shard_map/while/body/eval_jaxpr/ppermute | solution.py:12
  173.1 2.9 convolution_convert_fusion.3
  176.6 15.8 %collective-permute-done = f32[4,128,128]{2,0,1:T(4,128)S(1)} collective-permute-done((f32[4,128,128]{2,0,1:T(4,128)S(1)}, f32[4,128,128]{2,0,1:T(4,128)S(1)}, u32[]{:S(2)}, u32[]{:S(2)}) %collective-permute-start) | collective-permute-done | bytes 262176 | tf_op jit(solution)/shard_map/while/body/eval_jaxpr/ppermute | solution.py:12
  193.6 2.9 convolution_convert_fusion.3
  197.2 12.8 %collective-permute-done = f32[4,128,128]{2,0,1:T(4,128)S(1)} collective-permute-done((f32[4,128,128]{2,0,1:T(4,128)S(1)}, f32[4,128,128]{2,0,1:T(4,128)S(1)}, u32[]{:S(2)}, u32[]{:S(2)}) %collective-permute-start) | collective-permute-done | bytes 262176 | tf_op jit(solution)/shard_map/while/body/eval_jaxpr/ppermute | solution.py:12
  216.1 15.8 %collective-permute-done = f32[4,128,128]{2,0,1:T(4,128)S(1)} collective-permute-done((f32[4,128,128]{2,0,1:T(4,128)S(1)}, f32[4,128,128]{2,0,1:T(4,128)S(1)}, u32[]{:S(2)}, u32[]{:S(2)}) %collective-permute-start) | collective-permute-done | bytes 262176 | tf_op jit(solution)/shard_map/while/body/eval_jaxpr/ppermute | solution.py:12
  233.0 2.9 convolution_convert_fusion.3
  236.5 15.7 %collective-permute-done = f32[4,128,128]{2,0,1:T(4,128)S(1)} collective-permute-done((f32[4,128,128]{2,0,1:T(4,128)S(1)}, f32[4,128,128]{2,0,1:T(4,128)S(1)}, u32[]{:S(2)}, u32[]{:S(2)}) %collective-permute-start) | collective-permute-done | bytes 262176 | tf_op jit(solution)/shard_map/while/body/eval_jaxpr/ppermute | solution.py:12
  253.4 2.9 convolution_convert_fusion.3
  257.0 12.8 %collective-permute-done = f32[4,128,128]{2,0,1:T(4,128)S(1)} collective-permute-done((f32[4,128,128]{2,0,1:T(4,128)S(1)}, f32[4,128,128]{2,0,1:T(4,128)S(1)}, u32[]{:S(2)}, u32[]{:S(2)}) %collective-permute-start) | collective-permute-done | bytes 262176 | tf_op jit(solution)/shard_map/while/body/eval_jaxpr/ppermute | solution.py:12
  270.9 2.9 convolution_convert_fusion.3
  274.4 17.2 %collective-permute-done = f32[4,128,128]{2,0,1:T(4,128)S(1)} collective-permute-done((f32[4,128,128]{2,0,1:T(4,128)S(1)}, f32[4,128,128]{2,0,1:T(4,128)S(1)}, u32[]{:S(2)}, u32[]{:S(2)}) %collective-permute-start) | collective-permute-done | bytes 262176 | tf_op jit(solution)/shard_map/while/body/eval_jaxpr/ppermute | solution.py:12
  292.7 2.9 convolution_convert_fusion.3
  296.3 15.9 %collective-permute-done = f32[4,128,128]{2,0,1:T(4,128)S(1)} collective-permute-done((f32[4,128,128]{2,0,1:T(4,128)S(1)}, f32[4,128,128]{2,0,1:T(4,128)S(1)}, u32[]{:S(2)}, u32[]{:S(2)}) %collective-permute-start) | collective-permute-done | bytes 262176 | tf_op jit(solution)/shard_map/while/body/eval_jaxpr/ppermute | solution.py:12
  313.3 2.9 convolution_convert_fusion.3
  316.9 12.7 %collective-permute-done = f32[4,128,128]{2,0,1:T(4,128)S(1)} collective-permute-done((f32[4,128,128]{2,0,1:T(4,128)S(1)}, f32[4,128,128]{2,0,1:T(4,128)S(1)}, u32[]{:S(2)}, u32[]{:S(2)}) %collective-permute-start) | collective-permute-done | bytes 262176 | tf_op jit(solution)/shard_map/while/body/eval_jaxpr/ppermute | solution.py:12
  330.7 2.9 convolution_convert_fusion.3
  334.2 17.2 %collective-permute-done = f32[4,128,128]{2,0,1:T(4,128)S(1)} collective-permute-done((f32[4,128,128]{2,0,1:T(4,128)S(1)}, f32[4,128,128]{2,0,1:T(4,128)S(1)}, u32[]{:S(2)}, u32[]{:S(2)}) %collective-permute-start) | collective-permute-done | bytes 262176 | tf_op jit(solution)/shard_map/while/body/eval_jaxpr/ppermute | solution.py:12
  356.1 16.5 %collective-permute-done = f32[4,128,128]{2,0,1:T(4,128)S(1)} collective-permute-done((f32[4,128,128]{2,0,1:T(4,128)S(1)}, f32[4,128,128]{2,0,1:T(4,128)S(1)}, u32[]{:S(2)}, u32[]{:S(2)}) %collective-permute-start) | collective-permute-done | bytes 262176 | tf_op jit(solution)/shard_map/while/body/eval_jaxpr/ppermute | solution.py:12
  377.3 13.3 %collective-permute-done = f32[4,128,128]{2,0,1:T(4,128)S(1)} collective-permute-done((f32[4,128,128]{2,0,1:T(4,128)S(1)}, f32[4,128,128]{2,0,1:T(4,128)S(1)}, u32[]{:S(2)}, u32[]{:S(2)}) %collective-permute-start) | collective-permute-done | bytes 262176 | tf_op jit(solution)/shard_map/while/body/eval_jaxpr/ppermute | solution.py:12
  395.3 17.2 %collective-permute-done = f32[4,128,128]{2,0,1:T(4,128)S(1)} collective-permute-done((f32[4,128,128]{2,0,1:T(4,128)S(1)}, f32[4,128,128]{2,0,1:T(4,128)S(1)}, u32[]{:S(2)}, u32[]{:S(2)}) %collective-permute-start) | collective-permute-done | bytes 262176 | tf_op jit(solution)/shard_map/while/body/eval_jaxpr/ppermute | solution.py:12
  417.2 16.6 %collective-permute-done = f32[4,128,128]{2,0,1:T(4,128)S(1)} collective-permute-done((f32[4,128,128]{2,0,1:T(4,128)S(1)}, f32[4,128,128]{2,0,1:T(4,128)S(1)}, u32[]{:S(2)}, u32[]{:S(2)}) %collective-permute-start) | collective-permute-done | bytes 262176 | tf_op jit(solution)/shard_map/while/body/eval_jaxpr/ppermute | solution.py:12
  438.5 12.8 %collective-permute-done = f32[4,128,128]{2,0,1:T(4,128)S(1)} collective-permute-done((f32[4,128,128]{2,0,1:T(4,128)S(1)}, f32[4,128,128]{2,0,1:T(4,128)S(1)}, u32[]{:S(2)}, u32[]{:S(2)}) %collective-permute-start) | collective-permute-done | bytes 262176 | tf_op jit(solution)/shard_map/while/body/eval_jaxpr/ppermute | solution.py:12
  455.9 16.8 %collective-permute-done = f32[4,128,128]{2,0,1:T(4,128)S(1)} collective-permute-done((f32[4,128,128]{2,0,1:T(4,128)S(1)}, f32[4,128,128]{2,0,1:T(4,128)S(1)}, u32[]{:S(2)}, u32[]{:S(2)}) %collective-permute-start) | collective-permute-done | bytes 262176 | tf_op jit(solution)/shard_map/while/body/eval_jaxpr/ppermute | solution.py:12
  477.4 15.0 %collective-permute-done = f32[4,128,128]{2,0,1:T(4,128)S(1)} collective-permute-done((f32[4,128,128]{2,0,1:T(4,128)S(1)}, f32[4,128,128]{2,0,1:T(4,128)S(1)}, u32[]{:S(2)}, u32[]{:S(2)}) %collective-permute-start) | collective-permute-done | bytes 262176 | tf_op jit(solution)/shard_map/while/body/eval_jaxpr/ppermute | solution.py:12
  497.1 16.7 %collective-permute-done = f32[4,128,128]{2,0,1:T(4,128)S(1)} collective-permute-done((f32[4,128,128]{2,0,1:T(4,128)S(1)}, f32[4,128,128]{2,0,1:T(4,128)S(1)}, u32[]{:S(2)}, u32[]{:S(2)}) %collective-permute-start) | collective-permute-done | bytes 262176 | tf_op jit(solution)/shard_map/while/body/eval_jaxpr/ppermute | solution.py:12
  518.5 16.6 %collective-permute-done = f32[4,128,128]{2,0,1:T(4,128)S(1)} collective-permute-done((f32[4,128,128]{2,0,1:T(4,128)S(1)}, f32[4,128,128]{2,0,1:T(4,128)S(1)}, u32[]{:S(2)}, u32[]{:S(2)}) %collective-permute-start) | collective-permute-done | bytes 262176 | tf_op jit(solution)/shard_map/while/body/eval_jaxpr/ppermute | solution.py:12
  539.9 12.9 %collective-permute-done = f32[4,128,128]{2,0,1:T(4,128)S(1)} collective-permute-done((f32[4,128,128]{2,0,1:T(4,128)S(1)}, f32[4,128,128]{2,0,1:T(4,128)S(1)}, u32[]{:S(2)}, u32[]{:S(2)}) %collective-permute-start) | collective-permute-done | bytes 262176 | tf_op jit(solution)/shard_map/while/body/eval_jaxpr/ppermute | solution.py:12
  557.4 11.7 %collective-permute-done = f32[4,128,128]{2,0,1:T(4,128)S(1)} collective-permute-done((f32[4,128,128]{2,0,1:T(4,128)S(1)}, f32[4,128,128]{2,0,1:T(4,128)S(1)}, u32[]{:S(2)}, u32[]{:S(2)}) %collective-permute-start) | collective-permute-done | bytes 262176 | tf_op jit(solution)/shard_map/while/body/eval_jaxpr/ppermute | solution.py:12
  573.8 11.2 %collective-permute-done = f32[4,128,128]{2,0,1:T(4,128)S(1)} collective-permute-done((f32[4,128,128]{2,0,1:T(4,128)S(1)}, f32[4,128,128]{2,0,1:T(4,128)S(1)}, u32[]{:S(2)}, u32[]{:S(2)}) %collective-permute-start) | collective-permute-done | bytes 262176 | tf_op jit(solution)/shard_map/while/body/eval_jaxpr/ppermute | solution.py:12
  589.7 11.2 %collective-permute-done = f32[4,128,128]{2,0,1:T(4,128)S(1)} collective-permute-done((f32[4,128,128]{2,0,1:T(4,128)S(1)}, f32[4,128,128]{2,0,1:T(4,128)S(1)}, u32[]{:S(2)}, u32[]{:S(2)}) %collective-permute-start) | collective-permute-done | bytes 262176 | tf_op jit(solution)/shard_map/while/body/eval_jaxpr/ppermute | solution.py:12
  602.1 2.9 convolution_convert_fusion.3
  605.6 11.4 %collective-permute-done = f32[4,128,128]{2,0,1:T(4,128)S(1)} collective-permute-done((f32[4,128,128]{2,0,1:T(4,128)S(1)}, f32[4,128,128]{2,0,1:T(4,128)S(1)}, u32[]{:S(2)}, u32[]{:S(2)}) %collective-permute-start) | collective-permute-done | bytes 262176 | tf_op jit(solution)/shard_map/while/body/eval_jaxpr/ppermute | solution.py:12
  618.1 2.9 convolution_convert_fusion.3
  621.6 11.4 %collective-permute-done = f32[4,128,128]{2,0,1:T(4,128)S(1)} collective-permute-done((f32[4,128,128]{2,0,1:T(4,128)S(1)}, f32[4,128,128]{2,0,1:T(4,128)S(1)}, u32[]{:S(2)}, u32[]{:S(2)}) %collective-permute-start) | collective-permute-done | bytes 262176 | tf_op jit(solution)/shard_map/while/body/eval_jaxpr/ppermute | solution.py:12
  637.7 11.4 %collective-permute-done = f32[4,128,128]{2,0,1:T(4,128)S(1)} collective-permute-done((f32[4,128,128]{2,0,1:T(4,128)S(1)}, f32[4,128,128]{2,0,1:T(4,128)S(1)}, u32[]{:S(2)}, u32[]{:S(2)}) %collective-permute-start) | collective-permute-done | bytes 262176 | tf_op jit(solution)/shard_map/while/body/eval_jaxpr/ppermute | solution.py:12
  653.7 9.6 %collective-permute-done = f32[4,128,128]{2,0,1:T(4,128)S(1)} collective-permute-done((f32[4,128,128]{2,0,1:T(4,128)S(1)}, f32[4,128,128]{2,0,1:T(4,128)S(1)}, u32[]{:S(2)}, u32[]{:S(2)}) %collective-permute-start) | collective-permute-done | bytes 262176 | tf_op jit(solution)/shard_map/while/body/eval_jaxpr/ppermute | solution.py:12
  (313 shorter events, 115.4 us)
Async XLA Ops:
  6.5 56.0 %all-gather.2.cloned.1.call-start = ((), (), s32[]{:S(2)}) async-start(), calls=%async_computation | async-start | bytes 4718592 | tf_op jit(solution)/shard_map/all_gather | solution.py:16
  62.6 7.8 %copy-start = (bf16[128,128,128]{2,1,0:T(8,128)(2,1)S(1)}, bf16[128,128,128]{2,1,0:T(8,128)(2,1)}, u32[]{:S(2)}) copy-start(bf16[128,128,128]{2,1,0:T(8,128)(2,1)} %all-gather.2.cloned.1.call-done) | copy-start | bytes 12582916
  74.3 17.0 %collective-permute-start = (f32[4,128,128]{2,0,1:T(4,128)S(1)}, f32[4,128,128]{2,0,1:T(4,128)S(1)}, u32[]{:S(2)}, u32[]{:S(2)}) collective-permute-start(f32[4,128,128]{2,0,1:T(4,128)S(1)} %get-tuple-element.235), channel_id=1, source_target_pairs={{248,0},{0,8},{8,16},{16,24},{24,32},{32,40},{40,48},{48,56},{56,6... | collective-permute-start | bytes 786440 | tf_op jit(solution)/shard_map/while/body/eval_jaxpr/ppermute | solution.py:12
  92.2 19.7 %collective-permute-start = (f32[4,128,128]{2,0,1:T(4,128)S(1)}, f32[4,128,128]{2,0,1:T(4,128)S(1)}, u32[]{:S(2)}, u32[]{:S(2)}) collective-permute-start(f32[4,128,128]{2,0,1:T(4,128)S(1)} %get-tuple-element.235), channel_id=1, source_target_pairs={{248,0},{0,8},{8,16},{16,24},{24,32},{32,40},{40,48},{48,56},{56,6... | collective-permute-start | bytes 786440 | tf_op jit(solution)/shard_map/while/body/eval_jaxpr/ppermute | solution.py:12
  112.8 19.8 %collective-permute-start = (f32[4,128,128]{2,0,1:T(4,128)S(1)}, f32[4,128,128]{2,0,1:T(4,128)S(1)}, u32[]{:S(2)}, u32[]{:S(2)}) collective-permute-start(f32[4,128,128]{2,0,1:T(4,128)S(1)} %get-tuple-element.235), channel_id=1, source_target_pairs={{248,0},{0,8},{8,16},{16,24},{24,32},{32,40},{40,48},{48,56},{56,6... | collective-permute-start | bytes 786440 | tf_op jit(solution)/shard_map/while/body/eval_jaxpr/ppermute | solution.py:12
  133.6 16.6 %collective-permute-start = (f32[4,128,128]{2,0,1:T(4,128)S(1)}, f32[4,128,128]{2,0,1:T(4,128)S(1)}, u32[]{:S(2)}, u32[]{:S(2)}) collective-permute-start(f32[4,128,128]{2,0,1:T(4,128)S(1)} %get-tuple-element.235), channel_id=1, source_target_pairs={{248,0},{0,8},{8,16},{16,24},{24,32},{32,40},{40,48},{48,56},{56,6... | collective-permute-start | bytes 786440 | tf_op jit(solution)/shard_map/while/body/eval_jaxpr/ppermute | solution.py:12
  151.0 20.9 %collective-permute-start = (f32[4,128,128]{2,0,1:T(4,128)S(1)}, f32[4,128,128]{2,0,1:T(4,128)S(1)}, u32[]{:S(2)}, u32[]{:S(2)}) collective-permute-start(f32[4,128,128]{2,0,1:T(4,128)S(1)} %get-tuple-element.235), channel_id=1, source_target_pairs={{248,0},{0,8},{8,16},{16,24},{24,32},{32,40},{40,48},{48,56},{56,6... | collective-permute-start | bytes 786440 | tf_op jit(solution)/shard_map/while/body/eval_jaxpr/ppermute | solution.py:12
  172.9 19.6 %collective-permute-start = (f32[4,128,128]{2,0,1:T(4,128)S(1)}, f32[4,128,128]{2,0,1:T(4,128)S(1)}, u32[]{:S(2)}, u32[]{:S(2)}) collective-permute-start(f32[4,128,128]{2,0,1:T(4,128)S(1)} %get-tuple-element.235), channel_id=1, source_target_pairs={{248,0},{0,8},{8,16},{16,24},{24,32},{32,40},{40,48},{48,56},{56,6... | collective-permute-start | bytes 786440 | tf_op jit(solution)/shard_map/while/body/eval_jaxpr/ppermute | solution.py:12
  193.4 16.5 %collective-permute-start = (f32[4,128,128]{2,0,1:T(4,128)S(1)}, f32[4,128,128]{2,0,1:T(4,128)S(1)}, u32[]{:S(2)}, u32[]{:S(2)}) collective-permute-start(f32[4,128,128]{2,0,1:T(4,128)S(1)} %get-tuple-element.235), channel_id=1, source_target_pairs={{248,0},{0,8},{8,16},{16,24},{24,32},{32,40},{40,48},{48,56},{56,6... | collective-permute-start | bytes 786440 | tf_op jit(solution)/shard_map/while/body/eval_jaxpr/ppermute | solution.py:12
  210.9 21.0 %collective-permute-start = (f32[4,128,128]{2,0,1:T(4,128)S(1)}, f32[4,128,128]{2,0,1:T(4,128)S(1)}, u32[]{:S(2)}, u32[]{:S(2)}) collective-permute-start(f32[4,128,128]{2,0,1:T(4,128)S(1)} %get-tuple-element.235), channel_id=1, source_target_pairs={{248,0},{0,8},{8,16},{16,24},{24,32},{32,40},{40,48},{48,56},{56,6... | collective-permute-start | bytes 786440 | tf_op jit(solution)/shard_map/while/body/eval_jaxpr/ppermute | solution.py:12
  232.8 19.5 %collective-permute-start = (f32[4,128,128]{2,0,1:T(4,128)S(1)}, f32[4,128,128]{2,0,1:T(4,128)S(1)}, u32[]{:S(2)}, u32[]{:S(2)}) collective-permute-start(f32[4,128,128]{2,0,1:T(4,128)S(1)} %get-tuple-element.235), channel_id=1, source_target_pairs={{248,0},{0,8},{8,16},{16,24},{24,32},{32,40},{40,48},{48,56},{56,6... | collective-permute-start | bytes 786440 | tf_op jit(solution)/shard_map/while/body/eval_jaxpr/ppermute | solution.py:12
  253.2 16.5 %collective-permute-start = (f32[4,128,128]{2,0,1:T(4,128)S(1)}, f32[4,128,128]{2,0,1:T(4,128)S(1)}, u32[]{:S(2)}, u32[]{:S(2)}) collective-permute-start(f32[4,128,128]{2,0,1:T(4,128)S(1)} %get-tuple-element.235), channel_id=1, source_target_pairs={{248,0},{0,8},{8,16},{16,24},{24,32},{32,40},{40,48},{48,56},{56,6... | collective-permute-start | bytes 786440 | tf_op jit(solution)/shard_map/while/body/eval_jaxpr/ppermute | solution.py:12
  270.7 20.9 %collective-permute-start = (f32[4,128,128]{2,0,1:T(4,128)S(1)}, f32[4,128,128]{2,0,1:T(4,128)S(1)}, u32[]{:S(2)}, u32[]{:S(2)}) collective-permute-start(f32[4,128,128]{2,0,1:T(4,128)S(1)} %get-tuple-element.235), channel_id=1, source_target_pairs={{248,0},{0,8},{8,16},{16,24},{24,32},{32,40},{40,48},{48,56},{56,6... | collective-permute-start | bytes 786440 | tf_op jit(solution)/shard_map/while/body/eval_jaxpr/ppermute | solution.py:12
  292.5 19.7 %collective-permute-start = (f32[4,128,128]{2,0,1:T(4,128)S(1)}, f32[4,128,128]{2,0,1:T(4,128)S(1)}, u32[]{:S(2)}, u32[]{:S(2)}) collective-permute-start(f32[4,128,128]{2,0,1:T(4,128)S(1)} %get-tuple-element.235), channel_id=1, source_target_pairs={{248,0},{0,8},{8,16},{16,24},{24,32},{32,40},{40,48},{48,56},{56,6... | collective-permute-start | bytes 786440 | tf_op jit(solution)/shard_map/while/body/eval_jaxpr/ppermute | solution.py:12
  313.1 16.5 %collective-permute-start = (f32[4,128,128]{2,0,1:T(4,128)S(1)}, f32[4,128,128]{2,0,1:T(4,128)S(1)}, u32[]{:S(2)}, u32[]{:S(2)}) collective-permute-start(f32[4,128,128]{2,0,1:T(4,128)S(1)} %get-tuple-element.235), channel_id=1, source_target_pairs={{248,0},{0,8},{8,16},{16,24},{24,32},{32,40},{40,48},{48,56},{56,6... | collective-permute-start | bytes 786440 | tf_op jit(solution)/shard_map/while/body/eval_jaxpr/ppermute | solution.py:12
  330.5 20.9 %collective-permute-start = (f32[4,128,128]{2,0,1:T(4,128)S(1)}, f32[4,128,128]{2,0,1:T(4,128)S(1)}, u32[]{:S(2)}, u32[]{:S(2)}) collective-permute-start(f32[4,128,128]{2,0,1:T(4,128)S(1)} %get-tuple-element.235), channel_id=1, source_target_pairs={{248,0},{0,8},{8,16},{16,24},{24,32},{32,40},{40,48},{48,56},{56,6... | collective-permute-start | bytes 786440 | tf_op jit(solution)/shard_map/while/body/eval_jaxpr/ppermute | solution.py:12
  352.4 20.3 %collective-permute-start = (f32[4,128,128]{2,0,1:T(4,128)S(1)}, f32[4,128,128]{2,0,1:T(4,128)S(1)}, u32[]{:S(2)}, u32[]{:S(2)}) collective-permute-start(f32[4,128,128]{2,0,1:T(4,128)S(1)} %get-tuple-element.235), channel_id=1, source_target_pairs={{248,0},{0,8},{8,16},{16,24},{24,32},{32,40},{40,48},{48,56},{56,6... | collective-permute-start | bytes 786440 | tf_op jit(solution)/shard_map/while/body/eval_jaxpr/ppermute | solution.py:12
  373.6 17.1 %collective-permute-start = (f32[4,128,128]{2,0,1:T(4,128)S(1)}, f32[4,128,128]{2,0,1:T(4,128)S(1)}, u32[]{:S(2)}, u32[]{:S(2)}) collective-permute-start(f32[4,128,128]{2,0,1:T(4,128)S(1)} %get-tuple-element.235), channel_id=1, source_target_pairs={{248,0},{0,8},{8,16},{16,24},{24,32},{32,40},{40,48},{48,56},{56,6... | collective-permute-start | bytes 786440 | tf_op jit(solution)/shard_map/while/body/eval_jaxpr/ppermute | solution.py:12
  391.6 20.9 %collective-permute-start = (f32[4,128,128]{2,0,1:T(4,128)S(1)}, f32[4,128,128]{2,0,1:T(4,128)S(1)}, u32[]{:S(2)}, u32[]{:S(2)}) collective-permute-start(f32[4,128,128]{2,0,1:T(4,128)S(1)} %get-tuple-element.235), channel_id=1, source_target_pairs={{248,0},{0,8},{8,16},{16,24},{24,32},{32,40},{40,48},{48,56},{56,6... | collective-permute-start | bytes 786440 | tf_op jit(solution)/shard_map/while/body/eval_jaxpr/ppermute | solution.py:12
  413.4 20.4 %collective-permute-start = (f32[4,128,128]{2,0,1:T(4,128)S(1)}, f32[4,128,128]{2,0,1:T(4,128)S(1)}, u32[]{:S(2)}, u32[]{:S(2)}) collective-permute-start(f32[4,128,128]{2,0,1:T(4,128)S(1)} %get-tuple-element.235), channel_id=1, source_target_pairs={{248,0},{0,8},{8,16},{16,24},{24,32},{32,40},{40,48},{48,56},{56,6... | collective-permute-start | bytes 786440 | tf_op jit(solution)/shard_map/while/body/eval_jaxpr/ppermute | solution.py:12
  434.7 16.5 %collective-permute-start = (f32[4,128,128]{2,0,1:T(4,128)S(1)}, f32[4,128,128]{2,0,1:T(4,128)S(1)}, u32[]{:S(2)}, u32[]{:S(2)}) collective-permute-start(f32[4,128,128]{2,0,1:T(4,128)S(1)} %get-tuple-element.235), channel_id=1, source_target_pairs={{248,0},{0,8},{8,16},{16,24},{24,32},{32,40},{40,48},{48,56},{56,6... | collective-permute-start | bytes 786440 | tf_op jit(solution)/shard_map/while/body/eval_jaxpr/ppermute | solution.py:12
  452.2 20.6 %collective-permute-start = (f32[4,128,128]{2,0,1:T(4,128)S(1)}, f32[4,128,128]{2,0,1:T(4,128)S(1)}, u32[]{:S(2)}, u32[]{:S(2)}) collective-permute-start(f32[4,128,128]{2,0,1:T(4,128)S(1)} %get-tuple-element.235), channel_id=1, source_target_pairs={{248,0},{0,8},{8,16},{16,24},{24,32},{32,40},{40,48},{48,56},{56,6... | collective-permute-start | bytes 786440 | tf_op jit(solution)/shard_map/while/body/eval_jaxpr/ppermute | solution.py:12
  473.7 18.8 %collective-permute-start = (f32[4,128,128]{2,0,1:T(4,128)S(1)}, f32[4,128,128]{2,0,1:T(4,128)S(1)}, u32[]{:S(2)}, u32[]{:S(2)}) collective-permute-start(f32[4,128,128]{2,0,1:T(4,128)S(1)} %get-tuple-element.235), channel_id=1, source_target_pairs={{248,0},{0,8},{8,16},{16,24},{24,32},{32,40},{40,48},{48,56},{56,6... | collective-permute-start | bytes 786440 | tf_op jit(solution)/shard_map/while/body/eval_jaxpr/ppermute | solution.py:12
  493.3 20.5 %collective-permute-start = (f32[4,128,128]{2,0,1:T(4,128)S(1)}, f32[4,128,128]{2,0,1:T(4,128)S(1)}, u32[]{:S(2)}, u32[]{:S(2)}) collective-permute-start(f32[4,128,128]{2,0,1:T(4,128)S(1)} %get-tuple-element.235), channel_id=1, source_target_pairs={{248,0},{0,8},{8,16},{16,24},{24,32},{32,40},{40,48},{48,56},{56,6... | collective-permute-start | bytes 786440 | tf_op jit(solution)/shard_map/while/body/eval_jaxpr/ppermute | solution.py:12
  514.8 20.4 %collective-permute-start = (f32[4,128,128]{2,0,1:T(4,128)S(1)}, f32[4,128,128]{2,0,1:T(4,128)S(1)}, u32[]{:S(2)}, u32[]{:S(2)}) collective-permute-start(f32[4,128,128]{2,0,1:T(4,128)S(1)} %get-tuple-element.235), channel_id=1, source_target_pairs={{248,0},{0,8},{8,16},{16,24},{24,32},{32,40},{40,48},{48,56},{56,6... | collective-permute-start | bytes 786440 | tf_op jit(solution)/shard_map/while/body/eval_jaxpr/ppermute | solution.py:12
  536.1 16.7 %collective-permute-start = (f32[4,128,128]{2,0,1:T(4,128)S(1)}, f32[4,128,128]{2,0,1:T(4,128)S(1)}, u32[]{:S(2)}, u32[]{:S(2)}) collective-permute-start(f32[4,128,128]{2,0,1:T(4,128)S(1)} %get-tuple-element.235), channel_id=1, source_target_pairs={{248,0},{0,8},{8,16},{16,24},{24,32},{32,40},{40,48},{48,56},{56,6... | collective-permute-start | bytes 786440 | tf_op jit(solution)/shard_map/while/body/eval_jaxpr/ppermute | solution.py:12
  553.7 15.5 %collective-permute-start = (f32[4,128,128]{2,0,1:T(4,128)S(1)}, f32[4,128,128]{2,0,1:T(4,128)S(1)}, u32[]{:S(2)}, u32[]{:S(2)}) collective-permute-start(f32[4,128,128]{2,0,1:T(4,128)S(1)} %get-tuple-element.235), channel_id=1, source_target_pairs={{248,0},{0,8},{8,16},{16,24},{24,32},{32,40},{40,48},{48,56},{56,6... | collective-permute-start | bytes 786440 | tf_op jit(solution)/shard_map/while/body/eval_jaxpr/ppermute | solution.py:12
  570.1 15.0 %collective-permute-start = (f32[4,128,128]{2,0,1:T(4,128)S(1)}, f32[4,128,128]{2,0,1:T(4,128)S(1)}, u32[]{:S(2)}, u32[]{:S(2)}) collective-permute-start(f32[4,128,128]{2,0,1:T(4,128)S(1)} %get-tuple-element.235), channel_id=1, source_target_pairs={{248,0},{0,8},{8,16},{16,24},{24,32},{32,40},{40,48},{48,56},{56,6... | collective-permute-start | bytes 786440 | tf_op jit(solution)/shard_map/while/body/eval_jaxpr/ppermute | solution.py:12
  586.0 15.0 %collective-permute-start = (f32[4,128,128]{2,0,1:T(4,128)S(1)}, f32[4,128,128]{2,0,1:T(4,128)S(1)}, u32[]{:S(2)}, u32[]{:S(2)}) collective-permute-start(f32[4,128,128]{2,0,1:T(4,128)S(1)} %get-tuple-element.235), channel_id=1, source_target_pairs={{248,0},{0,8},{8,16},{16,24},{24,32},{32,40},{40,48},{48,56},{56,6... | collective-permute-start | bytes 786440 | tf_op jit(solution)/shard_map/while/body/eval_jaxpr/ppermute | solution.py:12
  601.8 15.1 %collective-permute-start = (f32[4,128,128]{2,0,1:T(4,128)S(1)}, f32[4,128,128]{2,0,1:T(4,128)S(1)}, u32[]{:S(2)}, u32[]{:S(2)}) collective-permute-start(f32[4,128,128]{2,0,1:T(4,128)S(1)} %get-tuple-element.235), channel_id=1, source_target_pairs={{248,0},{0,8},{8,16},{16,24},{24,32},{32,40},{40,48},{48,56},{56,6... | collective-permute-start | bytes 786440 | tf_op jit(solution)/shard_map/while/body/eval_jaxpr/ppermute | solution.py:12
  617.9 15.1 %collective-permute-start = (f32[4,128,128]{2,0,1:T(4,128)S(1)}, f32[4,128,128]{2,0,1:T(4,128)S(1)}, u32[]{:S(2)}, u32[]{:S(2)}) collective-permute-start(f32[4,128,128]{2,0,1:T(4,128)S(1)} %get-tuple-element.235), channel_id=1, source_target_pairs={{248,0},{0,8},{8,16},{16,24},{24,32},{32,40},{40,48},{48,56},{56,6... | collective-permute-start | bytes 786440 | tf_op jit(solution)/shard_map/while/body/eval_jaxpr/ppermute | solution.py:12
  633.9 15.1 %collective-permute-start = (f32[4,128,128]{2,0,1:T(4,128)S(1)}, f32[4,128,128]{2,0,1:T(4,128)S(1)}, u32[]{:S(2)}, u32[]{:S(2)}) collective-permute-start(f32[4,128,128]{2,0,1:T(4,128)S(1)} %get-tuple-element.235), channel_id=1, source_target_pairs={{248,0},{0,8},{8,16},{16,24},{24,32},{32,40},{40,48},{48,56},{56,6... | collective-permute-start | bytes 786440 | tf_op jit(solution)/shard_map/while/body/eval_jaxpr/ppermute | solution.py:12
  650.0 13.4 %collective-permute-start = (f32[4,128,128]{2,0,1:T(4,128)S(1)}, f32[4,128,128]{2,0,1:T(4,128)S(1)}, u32[]{:S(2)}, u32[]{:S(2)}) collective-permute-start(f32[4,128,128]{2,0,1:T(4,128)S(1)} %get-tuple-element.235), channel_id=1, source_target_pairs={{248,0},{0,8},{8,16},{16,24},{24,32},{32,40},{40,48},{48,56},{56,6... | collective-permute-start | bytes 786440 | tf_op jit(solution)/shard_map/while/body/eval_jaxpr/ppermute | solution.py:12
Sparse Core Ops, SparseCore 0:
  9.1 53.4 all-gather.1
where the time goes:
time: 673 us; the launch traced here: 672 us
  waiting for transfers between devices  493 us (73%)
  matrix products  131 us (19%)
  local copies, waits for them, and re-layouts  23.7 us (4%)
  between operations  13.4 us (2%)
    ppermute x31, waiting for transfers between devices, from_behind(): return lax.ppermute(block, axis, route)  441 us
    dot_general x32, matrix products, partial_value(): jnp.dot(one_hot, flat_panel, preferred_element_type=jnp.float32)  91.8 us
    all_gather x1, waiting for transfers between devices, per_device(): gathered = lax.all_gather(x_blocks, 'grp', axis=0, tiled=True)  50.7 us
    dot_general x32, matrix products, partial_value(): jnp.einsum('pc,pyz->cyz', selector, product, precision=lax.Precision.HIGH...  28.9 us
  transfers between devices with their start and end apart: 32, of which 32 were waited for; matrix products, arithmetic and copies ran while one was open for 17% of the time, Pallas kernels for 0%

commit v1 on v0

--- a/solution.py
+++ b/solution.py
@@ -13,7 +13,9 @@
 
 
 def per_device(x_blocks, pair_left, pair_right, pair_target):
-    gathered = lax.all_gather(x_blocks, "grp", axis=0, tiled=True)
+    gathered = jnp.concatenate(
+        lax.all_to_all(jnp.stack([x_blocks] * lax.axis_size("grp")), "grp", 0, 0), axis=0
+    )
     group_count = lax.axis_size("blk")
     left_all = pair_left[0, 0]
     right_all = pair_right[0, 0]

time: 673 us -> 652 us (0.969)
  the two profiles are of different devices: /device:TPU:120 before, /device:TPU:88 now
where the time goes in v1:
time: 652 us; the launch traced here: 651 us
  waiting for transfers between devices  442 us (68%)
  matrix products  133 us (20%)
  starting transfers between devices  46.2 us (7%)
  local copies, waits for them, and re-layouts  24.1 us (4%)
    ppermute x31, waiting for transfers between devices, from_behind(): return lax.ppermute(block, axis, route)  353 us
    dot_general x32, matrix products, partial_value(): jnp.dot(one_hot, flat_panel, preferred_element_type=jnp.float32)  94 us
    all_to_all x1, waiting for transfers between devices, per_device(): lax.all_to_all(jnp.stack([x_blocks] * lax.axis_size('grp')), 'grp', 0, 0)  89.5 us
    ppermute x31, starting transfers between devices, from_behind(): return lax.ppermute(block, axis, route)  40.5 us
    dot_general x32, matrix products, partial_value(): jnp.einsum('pc,pyz->cyz', selector, product, precision=lax.Precision.HIGH...  28.9 us
  transfers between devices with their start and end apart: 32, of which 32 were waited for; matrix products, arithmetic and copies ran while one was open for 17% of the time, Pallas kernels for 0%

profile of v1, /device:TPU:88, one launch (start us, length us, event | category | flops | bytes accessed | tf_op | source)
XLA Modules:
  0.0 650.6 jit_solution(9522943776988197377)
XLA Ops:
  0.0 4.0 stack.2
  4.0 5.7 all-to-all-start
  10.9 89.5 %all-to-all-done = bf16[8,16,128,128]{3,2,1,0:T(8,128)(2,1)} async-done(((bf16[8,16,128,128]{3,2,1,0:T(8,128)(2,1)}), bf16[8,16,128,128]{3,2,1,0:T(8,128)(2,1)}, u32[]{:S(2)}, u32[]{:S(2)}) %all-to-all-start) | async-done | bytes 4194336 | tf_op jit(solution)/shard_map/all_to_all | solution.py:17
  100.4 7.7 %copy.29 = bf16[16,8,128,128]{3,1,2,0:T(8,128)(2,1)} copy(bf16[16,8,128,128]{3,2,1,0:T(8,128)(2,1)} %bitcast.16) | data formatting | bytes 8388608
  108.1 4.5 convolution_convert_fusion.1
  114.2 535.7 %while.15 = (s32[]{:T(128)}, f32[4,128,128]{2,0,1:T(4,128)S(1)}, s32[32,12]{1,0:T(8,128)S(1)}, s32[32,12]{1,0:T(8,128)S(1)}, s32[32,12]{1,0:T(8,128)S(1)}, /*ind...) while((s32[]{:T(128)}, f32[4,128,128]{2,0,1:T(4,128)S(1)}, s32[32,12]{1,0:T(8,128)S(1)}, ...), condition=%wide.region_1.2_spmd, body=%wide.region_0.1_spmd.sunk | while | flops 160894032 | bytes 12583719 | solution.py:54
  114.2 5.8 collective-permute-start
  123.6 7.3 %collective-permute-done = f32[4,128,128]{2,0,1:T(4,128)S(1)} collective-permute-done((f32[4,128,128]{2,0,1:T(4,128)S(1)}, f32[4,128,128]{2,0,1:T(4,128)S(1)}, u32[]{:S(2)}, u32[]{:S(2)}) %collective-permute-start) | collective-permute-done | bytes 262176 | tf_op jit(solution)/shard_map/while/body/eval_jaxpr/ppermute | solution.py:12
  138.1 7.6 %collective-permute-done = f32[4,128,128]{2,0,1:T(4,128)S(1)} collective-permute-done((f32[4,128,128]{2,0,1:T(4,128)S(1)}, f32[4,128,128]{2,0,1:T(4,128)S(1)}, u32[]{:S(2)}, u32[]{:S(2)}) %collective-permute-start) | collective-permute-done | bytes 262176 | tf_op jit(solution)/shard_map/while/body/eval_jaxpr/ppermute | solution.py:12
  146.8 2.9 convolution_convert_fusion.3
  150.4 9.7 %collective-permute-done = f32[4,128,128]{2,0,1:T(4,128)S(1)} collective-permute-done((f32[4,128,128]{2,0,1:T(4,128)S(1)}, f32[4,128,128]{2,0,1:T(4,128)S(1)}, u32[]{:S(2)}, u32[]{:S(2)}) %collective-permute-start) | collective-permute-done | bytes 262176 | tf_op jit(solution)/shard_map/while/body/eval_jaxpr/ppermute | solution.py:12
  161.2 2.9 convolution_convert_fusion.3
  164.7 9.7 %collective-permute-done = f32[4,128,128]{2,0,1:T(4,128)S(1)} collective-permute-done((f32[4,128,128]{2,0,1:T(4,128)S(1)}, f32[4,128,128]{2,0,1:T(4,128)S(1)}, u32[]{:S(2)}, u32[]{:S(2)}) %collective-permute-start) | collective-permute-done | bytes 262176 | tf_op jit(solution)/shard_map/while/body/eval_jaxpr/ppermute | solution.py:12
  175.6 2.9 convolution_convert_fusion.3
  179.1 9.7 %collective-permute-done = f32[4,128,128]{2,0,1:T(4,128)S(1)} collective-permute-done((f32[4,128,128]{2,0,1:T(4,128)S(1)}, f32[4,128,128]{2,0,1:T(4,128)S(1)}, u32[]{:S(2)}, u32[]{:S(2)}) %collective-permute-start) | collective-permute-done | bytes 262176 | tf_op jit(solution)/shard_map/while/body/eval_jaxpr/ppermute | solution.py:12
  190.0 2.9 convolution_convert_fusion.3
  193.5 9.7 %collective-permute-done = f32[4,128,128]{2,0,1:T(4,128)S(1)} collective-permute-done((f32[4,128,128]{2,0,1:T(4,128)S(1)}, f32[4,128,128]{2,0,1:T(4,128)S(1)}, u32[]{:S(2)}, u32[]{:S(2)}) %collective-permute-start) | collective-permute-done | bytes 262176 | tf_op jit(solution)/shard_map/while/body/eval_jaxpr/ppermute | solution.py:12
  207.9 9.7 %collective-permute-done = f32[4,128,128]{2,0,1:T(4,128)S(1)} collective-permute-done((f32[4,128,128]{2,0,1:T(4,128)S(1)}, f32[4,128,128]{2,0,1:T(4,128)S(1)}, u32[]{:S(2)}, u32[]{:S(2)}) %collective-permute-start) | collective-permute-done | bytes 262176 | tf_op jit(solution)/shard_map/while/body/eval_jaxpr/ppermute | solution.py:12
  222.3 9.7 %collective-permute-done = f32[4,128,128]{2,0,1:T(4,128)S(1)} collective-permute-done((f32[4,128,128]{2,0,1:T(4,128)S(1)}, f32[4,128,128]{2,0,1:T(4,128)S(1)}, u32[]{:S(2)}, u32[]{:S(2)}) %collective-permute-start) | collective-permute-done | bytes 262176 | tf_op jit(solution)/shard_map/while/body/eval_jaxpr/ppermute | solution.py:12
  236.7 9.7 %collective-permute-done = f32[4,128,128]{2,0,1:T(4,128)S(1)} collective-permute-done((f32[4,128,128]{2,0,1:T(4,128)S(1)}, f32[4,128,128]{2,0,1:T(4,128)S(1)}, u32[]{:S(2)}, u32[]{:S(2)}) %collective-permute-start) | collective-permute-done | bytes 262176 | tf_op jit(solution)/shard_map/while/body/eval_jaxpr/ppermute | solution.py:12
  251.1 9.7 %collective-permute-done = f32[4,128,128]{2,0,1:T(4,128)S(1)} collective-permute-done((f32[4,128,128]{2,0,1:T(4,128)S(1)}, f32[4,128,128]{2,0,1:T(4,128)S(1)}, u32[]{:S(2)}, u32[]{:S(2)}) %collective-permute-start) | collective-permute-done | bytes 262176 | tf_op jit(solution)/shard_map/while/body/eval_jaxpr/ppermute | solution.py:12
  261.7 6.9 %collective-permute-start = (f32[4,128,128]{2,0,1:T(4,128)S(1)}, f32[4,128,128]{2,0,1:T(4,128)S(1)}, u32[]{:S(2)}, u32[]{:S(2)}) collective-permute-start(f32[4,128,128]{2,0,1:T(4,128)S(1)} %get-tuple-element.235), channel_id=1, source_target_pairs={{248,0},{0,8},{8,16},{16,24},{24,32},{32,40},{40,48},{48,56},{56,6... | collective-permute-start | bytes 786440 | tf_op jit(solution)/shard_map/while/body/eval_jaxpr/ppermute | solution.py:12
  272.3 5.9 collective-permute-done
  279.1 6.6 %collective-permute-start = (f32[4,128,128]{2,0,1:T(4,128)S(1)}, f32[4,128,128]{2,0,1:T(4,128)S(1)}, u32[]{:S(2)}, u32[]{:S(2)}) collective-permute-start(f32[4,128,128]{2,0,1:T(4,128)S(1)} %get-tuple-element.235), channel_id=1, source_target_pairs={{248,0},{0,8},{8,16},{16,24},{24,32},{32,40},{40,48},{48,56},{56,6... | collective-permute-start | bytes 786440 | tf_op jit(solution)/shard_map/while/body/eval_jaxpr/ppermute | solution.py:12
  289.3 9.8 %collective-permute-done = f32[4,128,128]{2,0,1:T(4,128)S(1)} collective-permute-done((f32[4,128,128]{2,0,1:T(4,128)S(1)}, f32[4,128,128]{2,0,1:T(4,128)S(1)}, u32[]{:S(2)}, u32[]{:S(2)}) %collective-permute-start) | collective-permute-done | bytes 262176 | tf_op jit(solution)/shard_map/while/body/eval_jaxpr/ppermute | solution.py:12
  300.0 9.9 %collective-permute-start = (f32[4,128,128]{2,0,1:T(4,128)S(1)}, f32[4,128,128]{2,0,1:T(4,128)S(1)}, u32[]{:S(2)}, u32[]{:S(2)}) collective-permute-start(f32[4,128,128]{2,0,1:T(4,128)S(1)} %get-tuple-element.235), channel_id=1, source_target_pairs={{248,0},{0,8},{8,16},{16,24},{24,32},{32,40},{40,48},{48,56},{56,6... | collective-permute-start | bytes 786440 | tf_op jit(solution)/shard_map/while/body/eval_jaxpr/ppermute | solution.py:12
  313.6 3.6 collective-permute-done
  318.1 6.6 %collective-permute-start = (f32[4,128,128]{2,0,1:T(4,128)S(1)}, f32[4,128,128]{2,0,1:T(4,128)S(1)}, u32[]{:S(2)}, u32[]{:S(2)}) collective-permute-start(f32[4,128,128]{2,0,1:T(4,128)S(1)} %get-tuple-element.235), channel_id=1, source_target_pairs={{248,0},{0,8},{8,16},{16,24},{24,32},{32,40},{40,48},{48,56},{56,6... | collective-permute-start | bytes 786440 | tf_op jit(solution)/shard_map/while/body/eval_jaxpr/ppermute | solution.py:12
  328.3 8.8 %collective-permute-done = f32[4,128,128]{2,0,1:T(4,128)S(1)} collective-permute-done((f32[4,128,128]{2,0,1:T(4,128)S(1)}, f32[4,128,128]{2,0,1:T(4,128)S(1)}, u32[]{:S(2)}, u32[]{:S(2)}) %collective-permute-start) | collective-permute-done | bytes 262176 | tf_op jit(solution)/shard_map/while/body/eval_jaxpr/ppermute | solution.py:12
  341.7 16.4 %collective-permute-done = f32[4,128,128]{2,0,1:T(4,128)S(1)} collective-permute-done((f32[4,128,128]{2,0,1:T(4,128)S(1)}, f32[4,128,128]{2,0,1:T(4,128)S(1)}, u32[]{:S(2)}, u32[]{:S(2)}) %collective-permute-start) | collective-permute-done | bytes 262176 | tf_op jit(solution)/shard_map/while/body/eval_jaxpr/ppermute | solution.py:12
  362.8 13.2 %collective-permute-done = f32[4,128,128]{2,0,1:T(4,128)S(1)} collective-permute-done((f32[4,128,128]{2,0,1:T(4,128)S(1)}, f32[4,128,128]{2,0,1:T(4,128)S(1)}, u32[]{:S(2)}, u32[]{:S(2)}) %collective-permute-start) | collective-permute-done | bytes 262176 | tf_op jit(solution)/shard_map/while/body/eval_jaxpr/ppermute | solution.py:12
  377.2 2.9 convolution_convert_fusion.3
  380.7 17.1 %collective-permute-done = f32[4,128,128]{2,0,1:T(4,128)S(1)} collective-permute-done((f32[4,128,128]{2,0,1:T(4,128)S(1)}, f32[4,128,128]{2,0,1:T(4,128)S(1)}, u32[]{:S(2)}, u32[]{:S(2)}) %collective-permute-start) | collective-permute-done | bytes 262176 | tf_op jit(solution)/shard_map/while/body/eval_jaxpr/ppermute | solution.py:12
  402.5 16.4 %collective-permute-done = f32[4,128,128]{2,0,1:T(4,128)S(1)} collective-permute-done((f32[4,128,128]{2,0,1:T(4,128)S(1)}, f32[4,128,128]{2,0,1:T(4,128)S(1)}, u32[]{:S(2)}, u32[]{:S(2)}) %collective-permute-start) | collective-permute-done | bytes 262176 | tf_op jit(solution)/shard_map/while/body/eval_jaxpr/ppermute | solution.py:12
  423.6 12.9 %collective-permute-done = f32[4,128,128]{2,0,1:T(4,128)S(1)} collective-permute-done((f32[4,128,128]{2,0,1:T(4,128)S(1)}, f32[4,128,128]{2,0,1:T(4,128)S(1)}, u32[]{:S(2)}, u32[]{:S(2)}) %collective-permute-start) | collective-permute-done | bytes 262176 | tf_op jit(solution)/shard_map/while/body/eval_jaxpr/ppermute | solution.py:12
  441.1 17.1 %collective-permute-done = f32[4,128,128]{2,0,1:T(4,128)S(1)} collective-permute-done((f32[4,128,128]{2,0,1:T(4,128)S(1)}, f32[4,128,128]{2,0,1:T(4,128)S(1)}, u32[]{:S(2)}, u32[]{:S(2)}) %collective-permute-start) | collective-permute-done | bytes 262176 | tf_op jit(solution)/shard_map/while/body/eval_jaxpr/ppermute | solution.py:12
  462.9 14.6 %collective-permute-done = f32[4,128,128]{2,0,1:T(4,128)S(1)} collective-permute-done((f32[4,128,128]{2,0,1:T(4,128)S(1)}, f32[4,128,128]{2,0,1:T(4,128)S(1)}, u32[]{:S(2)}, u32[]{:S(2)}) %collective-permute-start) | collective-permute-done | bytes 262176 | tf_op jit(solution)/shard_map/while/body/eval_jaxpr/ppermute | solution.py:12
  482.2 11.4 %collective-permute-done = f32[4,128,128]{2,0,1:T(4,128)S(1)} collective-permute-done((f32[4,128,128]{2,0,1:T(4,128)S(1)}, f32[4,128,128]{2,0,1:T(4,128)S(1)}, u32[]{:S(2)}, u32[]{:S(2)}) %collective-permute-start) | collective-permute-done | bytes 262176 | tf_op jit(solution)/shard_map/while/body/eval_jaxpr/ppermute | solution.py:12
  498.3 16.9 %collective-permute-done = f32[4,128,128]{2,0,1:T(4,128)S(1)} collective-permute-done((f32[4,128,128]{2,0,1:T(4,128)S(1)}, f32[4,128,128]{2,0,1:T(4,128)S(1)}, u32[]{:S(2)}, u32[]{:S(2)}) %collective-permute-start) | collective-permute-done | bytes 262176 | tf_op jit(solution)/shard_map/while/body/eval_jaxpr/ppermute | solution.py:12
  519.9 15.1 %collective-permute-done = f32[4,128,128]{2,0,1:T(4,128)S(1)} collective-permute-done((f32[4,128,128]{2,0,1:T(4,128)S(1)}, f32[4,128,128]{2,0,1:T(4,128)S(1)}, u32[]{:S(2)}, u32[]{:S(2)}) %collective-permute-start) | collective-permute-done | bytes 262176 | tf_op jit(solution)/shard_map/while/body/eval_jaxpr/ppermute | solution.py:12
  539.7 14.3 %collective-permute-done = f32[4,128,128]{2,0,1:T(4,128)S(1)} collective-permute-done((f32[4,128,128]{2,0,1:T(4,128)S(1)}, f32[4,128,128]{2,0,1:T(4,128)S(1)}, u32[]{:S(2)}, u32[]{:S(2)}) %collective-permute-start) | collective-permute-done | bytes 262176 | tf_op jit(solution)/shard_map/while/body/eval_jaxpr/ppermute | solution.py:12
  558.7 16.2 %collective-permute-done = f32[4,128,128]{2,0,1:T(4,128)S(1)} collective-permute-done((f32[4,128,128]{2,0,1:T(4,128)S(1)}, f32[4,128,128]{2,0,1:T(4,128)S(1)}, u32[]{:S(2)}, u32[]{:S(2)}) %collective-permute-start) | collective-permute-done | bytes 262176 | tf_op jit(solution)/shard_map/while/body/eval_jaxpr/ppermute | solution.py:12
  579.6 12.2 %collective-permute-done = f32[4,128,128]{2,0,1:T(4,128)S(1)} collective-permute-done((f32[4,128,128]{2,0,1:T(4,128)S(1)}, f32[4,128,128]{2,0,1:T(4,128)S(1)}, u32[]{:S(2)}, u32[]{:S(2)}) %collective-permute-start) | collective-permute-done | bytes 262176 | tf_op jit(solution)/shard_map/while/body/eval_jaxpr/ppermute | solution.py:12
  596.4 9.6 %collective-permute-done = f32[4,128,128]{2,0,1:T(4,128)S(1)} collective-permute-done((f32[4,128,128]{2,0,1:T(4,128)S(1)}, f32[4,128,128]{2,0,1:T(4,128)S(1)}, u32[]{:S(2)}, u32[]{:S(2)}) %collective-permute-start) | collective-permute-done | bytes 262176 | tf_op jit(solution)/shard_map/while/body/eval_jaxpr/ppermute | solution.py:12
  610.8 9.6 %collective-permute-done = f32[4,128,128]{2,0,1:T(4,128)S(1)} collective-permute-done((f32[4,128,128]{2,0,1:T(4,128)S(1)}, f32[4,128,128]{2,0,1:T(4,128)S(1)}, u32[]{:S(2)}, u32[]{:S(2)}) %collective-permute-start) | collective-permute-done | bytes 262176 | tf_op jit(solution)/shard_map/while/body/eval_jaxpr/ppermute | solution.py:12
  621.5 2.9 convolution_convert_fusion.3
  625.1 9.6 %collective-permute-done = f32[4,128,128]{2,0,1:T(4,128)S(1)} collective-permute-done((f32[4,128,128]{2,0,1:T(4,128)S(1)}, f32[4,128,128]{2,0,1:T(4,128)S(1)}, u32[]{:S(2)}, u32[]{:S(2)}) %collective-permute-start) | collective-permute-done | bytes 262176 | tf_op jit(solution)/shard_map/while/body/eval_jaxpr/ppermute | solution.py:12
  639.4 9.6 %collective-permute-done = f32[4,128,128]{2,0,1:T(4,128)S(1)} collective-permute-done((f32[4,128,128]{2,0,1:T(4,128)S(1)}, f32[4,128,128]{2,0,1:T(4,128)S(1)}, u32[]{:S(2)}, u32[]{:S(2)}) %collective-permute-start) | collective-permute-done | bytes 262176 | tf_op jit(solution)/shard_map/while/body/eval_jaxpr/ppermute | solution.py:12
  (317 shorter events, 130.8 us)
Async XLA Ops:
  4.0 5.7 copy-start.2
  4.0 5.8 copy-start.1
  4.0 5.9 copy-start
  4.0 96.4 %all-to-all-start = ((bf16[8,16,128,128]{3,2,1,0:T(8,128)(2,1)}), bf16[8,16,128,128]{3,2,1,0:T(8,128)(2,1)}, u32[]{:S(2)}, u32[]{:S(2)}) async-start(bf16[8,16,128,128]{3,2,1,0:T(8,128)(2,1)} %stack.2), calls=%async_computation | async-start | bytes 8388608 | tf_op jit(solution)/shard_map/all_to_all | solution.py:17
  114.2 16.7 %collective-permute-start = (f32[4,128,128]{2,0,1:T(4,128)S(1)}, f32[4,128,128]{2,0,1:T(4,128)S(1)}, u32[]{:S(2)}, u32[]{:S(2)}) collective-permute-start(f32[4,128,128]{2,0,1:T(4,128)S(1)} %get-tuple-element.235), channel_id=1, source_target_pairs={{248,0},{0,8},{8,16},{16,24},{24,32},{32,40},{40,48},{48,56},{56,6... | collective-permute-start | bytes 786440 | tf_op jit(solution)/shard_map/while/body/eval_jaxpr/ppermute | solution.py:12
  131.8 13.8 %collective-permute-start = (f32[4,128,128]{2,0,1:T(4,128)S(1)}, f32[4,128,128]{2,0,1:T(4,128)S(1)}, u32[]{:S(2)}, u32[]{:S(2)}) collective-permute-start(f32[4,128,128]{2,0,1:T(4,128)S(1)} %get-tuple-element.235), channel_id=1, source_target_pairs={{248,0},{0,8},{8,16},{16,24},{24,32},{32,40},{40,48},{48,56},{56,6... | collective-permute-start | bytes 786440 | tf_op jit(solution)/shard_map/while/body/eval_jaxpr/ppermute | solution.py:12
  146.6 13.5 %collective-permute-start = (f32[4,128,128]{2,0,1:T(4,128)S(1)}, f32[4,128,128]{2,0,1:T(4,128)S(1)}, u32[]{:S(2)}, u32[]{:S(2)}) collective-permute-start(f32[4,128,128]{2,0,1:T(4,128)S(1)} %get-tuple-element.235), channel_id=1, source_target_pairs={{248,0},{0,8},{8,16},{16,24},{24,32},{32,40},{40,48},{48,56},{56,6... | collective-permute-start | bytes 786440 | tf_op jit(solution)/shard_map/while/body/eval_jaxpr/ppermute | solution.py:12
  161.0 13.5 %collective-permute-start = (f32[4,128,128]{2,0,1:T(4,128)S(1)}, f32[4,128,128]{2,0,1:T(4,128)S(1)}, u32[]{:S(2)}, u32[]{:S(2)}) collective-permute-start(f32[4,128,128]{2,0,1:T(4,128)S(1)} %get-tuple-element.235), channel_id=1, source_target_pairs={{248,0},{0,8},{8,16},{16,24},{24,32},{32,40},{40,48},{48,56},{56,6... | collective-permute-start | bytes 786440 | tf_op jit(solution)/shard_map/while/body/eval_jaxpr/ppermute | solution.py:12
  175.4 13.5 %collective-permute-start = (f32[4,128,128]{2,0,1:T(4,128)S(1)}, f32[4,128,128]{2,0,1:T(4,128)S(1)}, u32[]{:S(2)}, u32[]{:S(2)}) collective-permute-start(f32[4,128,128]{2,0,1:T(4,128)S(1)} %get-tuple-element.235), channel_id=1, source_target_pairs={{248,0},{0,8},{8,16},{16,24},{24,32},{32,40},{40,48},{48,56},{56,6... | collective-permute-start | bytes 786440 | tf_op jit(solution)/shard_map/while/body/eval_jaxpr/ppermute | solution.py:12
  189.7 13.5 %collective-permute-start = (f32[4,128,128]{2,0,1:T(4,128)S(1)}, f32[4,128,128]{2,0,1:T(4,128)S(1)}, u32[]{:S(2)}, u32[]{:S(2)}) collective-permute-start(f32[4,128,128]{2,0,1:T(4,128)S(1)} %get-tuple-element.235), channel_id=1, source_target_pairs={{248,0},{0,8},{8,16},{16,24},{24,32},{32,40},{40,48},{48,56},{56,6... | collective-permute-start | bytes 786440 | tf_op jit(solution)/shard_map/while/body/eval_jaxpr/ppermute | solution.py:12
  204.1 13.5 %collective-permute-start = (f32[4,128,128]{2,0,1:T(4,128)S(1)}, f32[4,128,128]{2,0,1:T(4,128)S(1)}, u32[]{:S(2)}, u32[]{:S(2)}) collective-permute-start(f32[4,128,128]{2,0,1:T(4,128)S(1)} %get-tuple-element.235), channel_id=1, source_target_pairs={{248,0},{0,8},{8,16},{16,24},{24,32},{32,40},{40,48},{48,56},{56,6... | collective-permute-start | bytes 786440 | tf_op jit(solution)/shard_map/while/body/eval_jaxpr/ppermute | solution.py:12
  218.5 13.5 %collective-permute-start = (f32[4,128,128]{2,0,1:T(4,128)S(1)}, f32[4,128,128]{2,0,1:T(4,128)S(1)}, u32[]{:S(2)}, u32[]{:S(2)}) collective-permute-start(f32[4,128,128]{2,0,1:T(4,128)S(1)} %get-tuple-element.235), channel_id=1, source_target_pairs={{248,0},{0,8},{8,16},{16,24},{24,32},{32,40},{40,48},{48,56},{56,6... | collective-permute-start | bytes 786440 | tf_op jit(solution)/shard_map/while/body/eval_jaxpr/ppermute | solution.py:12
  232.9 13.5 %collective-permute-start = (f32[4,128,128]{2,0,1:T(4,128)S(1)}, f32[4,128,128]{2,0,1:T(4,128)S(1)}, u32[]{:S(2)}, u32[]{:S(2)}) collective-permute-start(f32[4,128,128]{2,0,1:T(4,128)S(1)} %get-tuple-element.235), channel_id=1, source_target_pairs={{248,0},{0,8},{8,16},{16,24},{24,32},{32,40},{40,48},{48,56},{56,6... | collective-permute-start | bytes 786440 | tf_op jit(solution)/shard_map/while/body/eval_jaxpr/ppermute | solution.py:12
  247.3 13.5 %collective-permute-start = (f32[4,128,128]{2,0,1:T(4,128)S(1)}, f32[4,128,128]{2,0,1:T(4,128)S(1)}, u32[]{:S(2)}, u32[]{:S(2)}) collective-permute-start(f32[4,128,128]{2,0,1:T(4,128)S(1)} %get-tuple-element.235), channel_id=1, source_target_pairs={{248,0},{0,8},{8,16},{16,24},{24,32},{32,40},{40,48},{48,56},{56,6... | collective-permute-start | bytes 786440 | tf_op jit(solution)/shard_map/while/body/eval_jaxpr/ppermute | solution.py:12
  261.7 16.4 %collective-permute-start = (f32[4,128,128]{2,0,1:T(4,128)S(1)}, f32[4,128,128]{2,0,1:T(4,128)S(1)}, u32[]{:S(2)}, u32[]{:S(2)}) collective-permute-start(f32[4,128,128]{2,0,1:T(4,128)S(1)} %get-tuple-element.235), channel_id=1, source_target_pairs={{248,0},{0,8},{8,16},{16,24},{24,32},{32,40},{40,48},{48,56},{56,6... | collective-permute-start | bytes 786440 | tf_op jit(solution)/shard_map/while/body/eval_jaxpr/ppermute | solution.py:12
  279.1 20.0 %collective-permute-start = (f32[4,128,128]{2,0,1:T(4,128)S(1)}, f32[4,128,128]{2,0,1:T(4,128)S(1)}, u32[]{:S(2)}, u32[]{:S(2)}) collective-permute-start(f32[4,128,128]{2,0,1:T(4,128)S(1)} %get-tuple-element.235), channel_id=1, source_target_pairs={{248,0},{0,8},{8,16},{16,24},{24,32},{32,40},{40,48},{48,56},{56,6... | collective-permute-start | bytes 786440 | tf_op jit(solution)/shard_map/while/body/eval_jaxpr/ppermute | solution.py:12
  300.0 17.2 %collective-permute-start = (f32[4,128,128]{2,0,1:T(4,128)S(1)}, f32[4,128,128]{2,0,1:T(4,128)S(1)}, u32[]{:S(2)}, u32[]{:S(2)}) collective-permute-start(f32[4,128,128]{2,0,1:T(4,128)S(1)} %get-tuple-element.235), channel_id=1, source_target_pairs={{248,0},{0,8},{8,16},{16,24},{24,32},{32,40},{40,48},{48,56},{56,6... | collective-permute-start | bytes 786440 | tf_op jit(solution)/shard_map/while/body/eval_jaxpr/ppermute | solution.py:12
  318.1 19.0 %collective-permute-start = (f32[4,128,128]{2,0,1:T(4,128)S(1)}, f32[4,128,128]{2,0,1:T(4,128)S(1)}, u32[]{:S(2)}, u32[]{:S(2)}) collective-permute-start(f32[4,128,128]{2,0,1:T(4,128)S(1)} %get-tuple-element.235), channel_id=1, source_target_pairs={{248,0},{0,8},{8,16},{16,24},{24,32},{32,40},{40,48},{48,56},{56,6... | collective-permute-start | bytes 786440 | tf_op jit(solution)/shard_map/while/body/eval_jaxpr/ppermute | solution.py:12
  338.0 20.2 %collective-permute-start = (f32[4,128,128]{2,0,1:T(4,128)S(1)}, f32[4,128,128]{2,0,1:T(4,128)S(1)}, u32[]{:S(2)}, u32[]{:S(2)}) collective-permute-start(f32[4,128,128]{2,0,1:T(4,128)S(1)} %get-tuple-element.235), channel_id=1, source_target_pairs={{248,0},{0,8},{8,16},{16,24},{24,32},{32,40},{40,48},{48,56},{56,6... | collective-permute-start | bytes 786440 | tf_op jit(solution)/shard_map/while/body/eval_jaxpr/ppermute | solution.py:12
  359.1 17.0 %collective-permute-start = (f32[4,128,128]{2,0,1:T(4,128)S(1)}, f32[4,128,128]{2,0,1:T(4,128)S(1)}, u32[]{:S(2)}, u32[]{:S(2)}) collective-permute-start(f32[4,128,128]{2,0,1:T(4,128)S(1)} %get-tuple-element.235), channel_id=1, source_target_pairs={{248,0},{0,8},{8,16},{16,24},{24,32},{32,40},{40,48},{48,56},{56,6... | collective-permute-start | bytes 786440 | tf_op jit(solution)/shard_map/while/body/eval_jaxpr/ppermute | solution.py:12
  377.0 20.9 %collective-permute-start = (f32[4,128,128]{2,0,1:T(4,128)S(1)}, f32[4,128,128]{2,0,1:T(4,128)S(1)}, u32[]{:S(2)}, u32[]{:S(2)}) collective-permute-start(f32[4,128,128]{2,0,1:T(4,128)S(1)} %get-tuple-element.235), channel_id=1, source_target_pairs={{248,0},{0,8},{8,16},{16,24},{24,32},{32,40},{40,48},{48,56},{56,6... | collective-permute-start | bytes 786440 | tf_op jit(solution)/shard_map/while/body/eval_jaxpr/ppermute | solution.py:12
  398.7 20.2 %collective-permute-start = (f32[4,128,128]{2,0,1:T(4,128)S(1)}, f32[4,128,128]{2,0,1:T(4,128)S(1)}, u32[]{:S(2)}, u32[]{:S(2)}) collective-permute-start(f32[4,128,128]{2,0,1:T(4,128)S(1)} %get-tuple-element.235), channel_id=1, source_target_pairs={{248,0},{0,8},{8,16},{16,24},{24,32},{32,40},{40,48},{48,56},{56,6... | collective-permute-start | bytes 786440 | tf_op jit(solution)/shard_map/while/body/eval_jaxpr/ppermute | solution.py:12
  419.8 16.6 %collective-permute-start = (f32[4,128,128]{2,0,1:T(4,128)S(1)}, f32[4,128,128]{2,0,1:T(4,128)S(1)}, u32[]{:S(2)}, u32[]{:S(2)}) collective-permute-start(f32[4,128,128]{2,0,1:T(4,128)S(1)} %get-tuple-element.235), channel_id=1, source_target_pairs={{248,0},{0,8},{8,16},{16,24},{24,32},{32,40},{40,48},{48,56},{56,6... | collective-permute-start | bytes 786440 | tf_op jit(solution)/shard_map/while/body/eval_jaxpr/ppermute | solution.py:12
  437.4 20.9 %collective-permute-start = (f32[4,128,128]{2,0,1:T(4,128)S(1)}, f32[4,128,128]{2,0,1:T(4,128)S(1)}, u32[]{:S(2)}, u32[]{:S(2)}) collective-permute-start(f32[4,128,128]{2,0,1:T(4,128)S(1)} %get-tuple-element.235), channel_id=1, source_target_pairs={{248,0},{0,8},{8,16},{16,24},{24,32},{32,40},{40,48},{48,56},{56,6... | collective-permute-start | bytes 786440 | tf_op jit(solution)/shard_map/while/body/eval_jaxpr/ppermute | solution.py:12
  459.2 18.4 %collective-permute-start = (f32[4,128,128]{2,0,1:T(4,128)S(1)}, f32[4,128,128]{2,0,1:T(4,128)S(1)}, u32[]{:S(2)}, u32[]{:S(2)}) collective-permute-start(f32[4,128,128]{2,0,1:T(4,128)S(1)} %get-tuple-element.235), channel_id=1, source_target_pairs={{248,0},{0,8},{8,16},{16,24},{24,32},{32,40},{40,48},{48,56},{56,6... | collective-permute-start | bytes 786440 | tf_op jit(solution)/shard_map/while/body/eval_jaxpr/ppermute | solution.py:12
  478.5 15.2 %collective-permute-start = (f32[4,128,128]{2,0,1:T(4,128)S(1)}, f32[4,128,128]{2,0,1:T(4,128)S(1)}, u32[]{:S(2)}, u32[]{:S(2)}) collective-permute-start(f32[4,128,128]{2,0,1:T(4,128)S(1)} %get-tuple-element.235), channel_id=1, source_target_pairs={{248,0},{0,8},{8,16},{16,24},{24,32},{32,40},{40,48},{48,56},{56,6... | collective-permute-start | bytes 786440 | tf_op jit(solution)/shard_map/while/body/eval_jaxpr/ppermute | solution.py:12
  494.6 20.6 %collective-permute-start = (f32[4,128,128]{2,0,1:T(4,128)S(1)}, f32[4,128,128]{2,0,1:T(4,128)S(1)}, u32[]{:S(2)}, u32[]{:S(2)}) collective-permute-start(f32[4,128,128]{2,0,1:T(4,128)S(1)} %get-tuple-element.235), channel_id=1, source_target_pairs={{248,0},{0,8},{8,16},{16,24},{24,32},{32,40},{40,48},{48,56},{56,6... | collective-permute-start | bytes 786440 | tf_op jit(solution)/shard_map/while/body/eval_jaxpr/ppermute | solution.py:12
  516.1 18.8 %collective-permute-start = (f32[4,128,128]{2,0,1:T(4,128)S(1)}, f32[4,128,128]{2,0,1:T(4,128)S(1)}, u32[]{:S(2)}, u32[]{:S(2)}) collective-permute-start(f32[4,128,128]{2,0,1:T(4,128)S(1)} %get-tuple-element.235), channel_id=1, source_target_pairs={{248,0},{0,8},{8,16},{16,24},{24,32},{32,40},{40,48},{48,56},{56,6... | collective-permute-start | bytes 786440 | tf_op jit(solution)/shard_map/while/body/eval_jaxpr/ppermute | solution.py:12
  535.9 18.1 %collective-permute-start = (f32[4,128,128]{2,0,1:T(4,128)S(1)}, f32[4,128,128]{2,0,1:T(4,128)S(1)}, u32[]{:S(2)}, u32[]{:S(2)}) collective-permute-start(f32[4,128,128]{2,0,1:T(4,128)S(1)} %get-tuple-element.235), channel_id=1, source_target_pairs={{248,0},{0,8},{8,16},{16,24},{24,32},{32,40},{40,48},{48,56},{56,6... | collective-permute-start | bytes 786440 | tf_op jit(solution)/shard_map/while/body/eval_jaxpr/ppermute | solution.py:12
  554.9 20.0 %collective-permute-start = (f32[4,128,128]{2,0,1:T(4,128)S(1)}, f32[4,128,128]{2,0,1:T(4,128)S(1)}, u32[]{:S(2)}, u32[]{:S(2)}) collective-permute-start(f32[4,128,128]{2,0,1:T(4,128)S(1)} %get-tuple-element.235), channel_id=1, source_target_pairs={{248,0},{0,8},{8,16},{16,24},{24,32},{32,40},{40,48},{48,56},{56,6... | collective-permute-start | bytes 786440 | tf_op jit(solution)/shard_map/while/body/eval_jaxpr/ppermute | solution.py:12
  575.8 16.0 %collective-permute-start = (f32[4,128,128]{2,0,1:T(4,128)S(1)}, f32[4,128,128]{2,0,1:T(4,128)S(1)}, u32[]{:S(2)}, u32[]{:S(2)}) collective-permute-start(f32[4,128,128]{2,0,1:T(4,128)S(1)} %get-tuple-element.235), channel_id=1, source_target_pairs={{248,0},{0,8},{8,16},{16,24},{24,32},{32,40},{40,48},{48,56},{56,6... | collective-permute-start | bytes 786440 | tf_op jit(solution)/shard_map/while/body/eval_jaxpr/ppermute | solution.py:12
  592.7 13.4 %collective-permute-start = (f32[4,128,128]{2,0,1:T(4,128)S(1)}, f32[4,128,128]{2,0,1:T(4,128)S(1)}, u32[]{:S(2)}, u32[]{:S(2)}) collective-permute-start(f32[4,128,128]{2,0,1:T(4,128)S(1)} %get-tuple-element.235), channel_id=1, source_target_pairs={{248,0},{0,8},{8,16},{16,24},{24,32},{32,40},{40,48},{48,56},{56,6... | collective-permute-start | bytes 786440 | tf_op jit(solution)/shard_map/while/body/eval_jaxpr/ppermute | solution.py:12
  607.0 13.4 %collective-permute-start = (f32[4,128,128]{2,0,1:T(4,128)S(1)}, f32[4,128,128]{2,0,1:T(4,128)S(1)}, u32[]{:S(2)}, u32[]{:S(2)}) collective-permute-start(f32[4,128,128]{2,0,1:T(4,128)S(1)} %get-tuple-element.235), channel_id=1, source_target_pairs={{248,0},{0,8},{8,16},{16,24},{24,32},{32,40},{40,48},{48,56},{56,6... | collective-permute-start | bytes 786440 | tf_op jit(solution)/shard_map/while/body/eval_jaxpr/ppermute | solution.py:12
  621.3 13.4 %collective-permute-start = (f32[4,128,128]{2,0,1:T(4,128)S(1)}, f32[4,128,128]{2,0,1:T(4,128)S(1)}, u32[]{:S(2)}, u32[]{:S(2)}) collective-permute-start(f32[4,128,128]{2,0,1:T(4,128)S(1)} %get-tuple-element.235), channel_id=1, source_target_pairs={{248,0},{0,8},{8,16},{16,24},{24,32},{32,40},{40,48},{48,56},{56,6... | collective-permute-start | bytes 786440 | tf_op jit(solution)/shard_map/while/body/eval_jaxpr/ppermute | solution.py:12
  635.6 13.4 %collective-permute-start = (f32[4,128,128]{2,0,1:T(4,128)S(1)}, f32[4,128,128]{2,0,1:T(4,128)S(1)}, u32[]{:S(2)}, u32[]{:S(2)}) collective-permute-start(f32[4,128,128]{2,0,1:T(4,128)S(1)} %get-tuple-element.235), channel_id=1, source_target_pairs={{248,0},{0,8},{8,16},{16,24},{24,32},{32,40},{40,48},{48,56},{56,6... | collective-permute-start | bytes 786440 | tf_op jit(solution)/shard_map/while/body/eval_jaxpr/ppermute | solution.py:12
